TPU v7x, 32 devices: a whole 2x2x4 slice. The times are simulated.
32 devices in a mesh: seq: 4 (over y, x), exp: 8 (over z, core).
Axes of the slice: x: 2, y: 2, z: 4, core: 2. Of those that a mesh axis runs over, the one named last changes fastest.
Arguments:
- token_ids: int32 [4, 32], replicated, may hold values from 0 to 51199
- cache_lengths: int32 [32], replicated, may hold values from 1 to 1024, as said below
- empty_blocks: int32 [32, 64], replicated, may hold values 0 or 1
- expert_ids: int32 [4, 32, 6], replicated, may hold values from 0 to 63, all different within a row
- embed_table: bfloat16 [51200, 2048], P(('seq', 'exp')), may hold values from -3 to 3
- attn_gain: float32 [2048], replicated, may hold values from 0.5 to 1.5
- w_query: bfloat16 [2048, 2048], P(None, 'seq'), may hold values from -0.125 to 0.125
- w_key: bfloat16 [2048, 2048], P(None, 'seq'), may hold values from -0.125 to 0.125
- w_value: bfloat16 [2048, 2048], P(None, 'seq'), may hold values from -0.125 to 0.125
- w_out: bfloat16 [2048, 2048], P('seq'), may hold values from -0.125 to 0.125
- k_cache: bfloat16 [32, 1024, 2048], P('exp', 'seq'), may hold values from -200 to 200
- v_cache: bfloat16 [32, 1024, 2048], P('exp', 'seq'), may hold values from -6 to 6
- moe_gain: float32 [2048], replicated, may hold values from 0.5 to 1.5
- w_router: bfloat16 [2048, 64], replicated, may hold values from -0.125 to 0.125
- gate_pieces: bfloat16 [256, 2048, 352], P(('seq', 'exp')), may hold values from -0.125 to 0.125
- up_pieces: bfloat16 [256, 2048, 352], P(('seq', 'exp')), may hold values from -0.125 to 0.125
- down_pieces: bfloat16 [256, 352, 2048], P(('seq', 'exp')), may hold values from -0.15625 to 0.15625
- shared_gate: bfloat16 [2048, 2816], P(None, 'exp'), may hold values from -0.125 to 0.125
- shared_up: bfloat16 [2048, 2816], P(None, 'exp'), may hold values from -0.125 to 0.125
- shared_down: bfloat16 [2816, 2048], P('exp'), may hold values from -0.109375 to 0.109375
- final_gain: float32 [2048], replicated, may hold values from 0.5 to 1.5
- w_head: bfloat16 [2048, 51200], P(None, ('seq', 'exp')), may hold values from -0.125 to 0.125
Outputs:
- hidden_norms: float32 [4, 32], replicated
- greatest_logits: float32 [4, 32], replicated
Inputs may be any that keep to these rules, and one draw needn't show every extreme that they name: `cache_lengths`: one of the 32 requests has exactly 1024 cached positions in every draw.
All inputs are finite; a program needn't handle non-finite values.
Results may differ from a plain program's by a relative error of at most 0.0055.
Values may be sent and summed in bfloat16 or wider, within the bound.
No kernel may reach another device: no remote copies, remote signals or barrier semaphores. Data moves between devices by JAX's collectives and lax.ppermute only.
A program may use at most 128 MiB of HBM per device.

v0:
```python
import math
import jax
import jax.numpy as jnp
from jax import lax
from jax.sharding import PartitionSpec as P

HDIM = 128
PIECES = 4
BLK = 16
epsilon = 1e-06
negative = -1e30


def rms_scale(values, scales):
    return values * lax.rsqrt(jnp.mean(values * values, axis=-1, keepdims=True) + epsilon) * scales


def rotate(values, places):
    half_width = values.shape[-1] // 2
    frequency = 10000.0 ** (-2.0 * jnp.arange(half_width, dtype=jnp.float32) / values.shape[-1])
    angles = places.astype(jnp.float32)[..., None, None] * frequency
    cosine_table = jnp.cos(angles)
    sine_table = jnp.sin(angles)
    lower = values[..., :half_width]
    upper = values[..., half_width:]
    return jnp.concatenate(
        [lower * cosine_table - upper * sine_table, upper * cosine_table + lower * sine_table],
        axis=-1,
    )


def joined(earlier, later):
    top_score = jnp.maximum(earlier[0], later[0])
    left_factor = jnp.exp(earlier[0] - top_score)
    right_factor = jnp.exp(later[0] - top_score)
    return (
        top_score,
        earlier[1] * left_factor + later[1] * right_factor,
        earlier[2] * left_factor[..., None] + later[2] * right_factor[..., None],
    )


def on_device(
    token_ids,
    cache_lengths,
    empty_blocks,
    expert_ids,
    embed_table,
    attn_gain,
    w_query,
    w_key,
    w_value,
    w_out,
    k_cache,
    v_cache,
    moe_gain,
    w_router,
    gate_pieces,
    up_pieces,
    down_pieces,
    shared_gate,
    shared_up,
    shared_down,
    final_gain,
    w_head,
):
    steps, requests = token_ids.shape
    tokens = steps * requests
    width = embed_table.shape[1]
    vocab_local = embed_table.shape[0]
    owner_index = lax.axis_index(("seq", "exp"))
    seq_index = lax.axis_index("seq")
    own_count = requests // lax.axis_size("exp")
    own_start = lax.axis_index("exp") * own_count
    local_ids = token_ids.reshape(tokens) - owner_index * vocab_local
    onehot = (local_ids[:, None] == jnp.arange(vocab_local, dtype=jnp.int32)[None, :]).astype(
        jnp.bfloat16
    )
    looked = jnp.dot(onehot, embed_table, preferred_element_type=jnp.float32).reshape(
        steps, requests, width
    )
    block_part = lax.psum_scatter(
        looked.astype(jnp.bfloat16), "exp", scatter_dimension=1, tiled=True
    )
    own_rows = lax.psum(block_part, "seq").astype(jnp.float32).reshape(steps * own_count, width)
    attn_in = rms_scale(own_rows, attn_gain).astype(jnp.bfloat16)
    own_lengths = lax.dynamic_slice_in_dim(cache_lengths, own_start, own_count, 0)
    places = (own_lengths[None, :] + jnp.arange(steps, dtype=jnp.int32)[:, None]).reshape(
        steps * own_count
    )
    heads_here = w_query.shape[1] // HDIM

    def project(weight):
        return jnp.dot(attn_in, weight, preferred_element_type=jnp.float32).reshape(
            steps * own_count, heads_here, HDIM
        )

    query_part = rotate(project(w_query), places).astype(jnp.bfloat16)
    key_part = rotate(project(w_key), places).astype(jnp.bfloat16)
    value_part = project(w_value).astype(jnp.bfloat16)
    queries, new_keys, new_values = (
        lax.all_gather(query_part, "seq", axis=1, tiled=True),
        lax.all_gather(key_part, "seq", axis=1, tiled=True),
        lax.all_gather(value_part, "seq", axis=1, tiled=True),
    )
    head_count = queries.shape[1]
    queries = queries.reshape(steps, own_count, head_count, HDIM)
    new_keys = new_keys.reshape(steps, own_count, head_count, HDIM)
    new_values = new_values.reshape(steps, own_count, head_count, HDIM)
    span = k_cache.shape[1]
    first_place = seq_index * span
    places_here = first_place + jnp.arange(span, dtype=jnp.int32)
    own_empty = lax.dynamic_slice_in_dim(empty_blocks, own_start, own_count, 0)
    local_blocks = lax.dynamic_slice_in_dim(own_empty, first_place // BLK, span // BLK, 1)
    blocked = jnp.broadcast_to(local_blocks[:, :, None], (own_count, span // BLK, BLK)).reshape(
        own_count, span
    )
    live_mask = ((places_here[None, :] < own_lengths[:, None]) & (blocked == 0))[None, :, None, :]
    cache_keys = k_cache.reshape(own_count, span, head_count, HDIM)
    cache_values = v_cache.reshape(own_count, span, head_count, HDIM)
    score_scale = 1.0 / math.sqrt(HDIM)
    cached = (
        jnp.einsum("trhd,rphd->trhp", queries, cache_keys, preferred_element_type=jnp.float32)
        * score_scale
    )
    local_top = jnp.max(jnp.where(live_mask, cached, negative), axis=3)
    top_score = lax.pmax(local_top, "seq")
    local_weights = jnp.where(live_mask, jnp.exp(cached - top_score[..., None]), 0.0)
    local_mixture = jnp.einsum(
        "trhp,rphd->trhd",
        local_weights.astype(jnp.bfloat16),
        cache_values,
        preferred_element_type=jnp.float32,
    )
    totals, mixture = (
        lax.psum(jnp.sum(local_weights, axis=3).astype(jnp.bfloat16), "seq").astype(jnp.float32),
        lax.psum(local_mixture.astype(jnp.bfloat16), "seq").astype(jnp.float32),
    )
    fresh_scores = (
        jnp.einsum("trhd,urhd->trhu", queries, new_keys, preferred_element_type=jnp.float32)
        * score_scale
    )
    causal = (jnp.arange(steps)[None, :] <= jnp.arange(steps)[:, None])[:, None, None, :]
    fresh_top = jnp.max(jnp.where(causal, fresh_scores, negative), axis=3)
    fresh_weights = jnp.where(causal, jnp.exp(fresh_scores - fresh_top[..., None]), 0.0)
    fresh_mixture = jnp.einsum(
        "trhu,urhd->trhd",
        fresh_weights.astype(jnp.bfloat16),
        new_values,
        preferred_element_type=jnp.float32,
    )
    top_score, totals, mixture = joined(
        (top_score, totals, mixture), (fresh_top, jnp.sum(fresh_weights, axis=3), fresh_mixture)
    )
    heads_out = (mixture / totals[..., None]).astype(jnp.bfloat16)
    own_heads = lax.dynamic_slice_in_dim(heads_out, seq_index * heads_here, heads_here, 2).reshape(
        steps * own_count, heads_here * HDIM
    )
    attn_sum = lax.psum(
        jnp.dot(own_heads, w_out, preferred_element_type=jnp.float32).astype(jnp.bfloat16), "seq"
    ).astype(jnp.float32)
    resid_own = own_rows + attn_sum
    resid_all = (
        lax.all_gather(
            resid_own.reshape(steps, own_count, width).astype(jnp.bfloat16),
            "exp",
            axis=1,
            tiled=True,
        )
        .astype(jnp.float32)
        .reshape(tokens, width)
    )
    moe_in = rms_scale(resid_all, moe_gain).astype(jnp.bfloat16)
    router = jax.nn.sigmoid(jnp.dot(moe_in, w_router, preferred_element_type=jnp.float32))
    expert_count = w_router.shape[1]
    chosen_ids = expert_ids.reshape(tokens, expert_ids.shape[2])
    picked = chosen_ids[:, :, None] == jnp.arange(expert_count, dtype=jnp.int32)[None, None, :]
    chosen = jnp.sum(jnp.where(picked, router[:, None, :], 0.0), axis=2)
    gate_weights = chosen / jnp.sum(chosen, axis=1, keepdims=True)
    rows_here = gate_pieces.shape[0]
    row_expert = (owner_index * rows_here + jnp.arange(rows_here, dtype=jnp.int32)) // PIECES
    token_weight = jnp.sum(
        jnp.where(
            chosen_ids[None, :, :] == row_expert[:, None, None], gate_weights[None, :, :], 0.0
        ),
        axis=2,
    )
    gate_out = jnp.einsum("nd,jdf->jnf", moe_in, gate_pieces, preferred_element_type=jnp.float32)
    up_out = jnp.einsum("nd,jdf->jnf", moe_in, up_pieces, preferred_element_type=jnp.float32)
    expert_hidden = (jax.nn.silu(gate_out) * up_out).astype(jnp.bfloat16)
    expert_out = jnp.einsum(
        "jnf,jfd->jnd", expert_hidden, down_pieces, preferred_element_type=jnp.float32
    )
    routed = jnp.einsum("jn,jnd->nd", token_weight, expert_out)
    share_count = tokens // lax.axis_size("seq")
    share_start = seq_index * share_count
    share_rows = lax.dynamic_slice_in_dim(moe_in, share_start, share_count, 0)
    shared_hidden = (
        jax.nn.silu(jnp.dot(share_rows, shared_gate, preferred_element_type=jnp.float32))
        * jnp.dot(share_rows, shared_up, preferred_element_type=jnp.float32)
    ).astype(jnp.bfloat16)
    shared_out = jnp.dot(shared_hidden, shared_down, preferred_element_type=jnp.float32)
    term_rows = lax.dynamic_update_slice_in_dim(
        routed,
        lax.dynamic_slice_in_dim(routed, share_start, share_count, 0) + shared_out,
        share_start,
        0,
    )
    final_hidden = resid_all + lax.psum(term_rows, ("seq", "exp"))
    hidden_norms = jnp.sqrt(jnp.mean(final_hidden * final_hidden, axis=-1)).reshape(steps, requests)
    head_in = rms_scale(final_hidden, final_gain).astype(jnp.bfloat16)
    local_best = jnp.max(jnp.dot(head_in, w_head, preferred_element_type=jnp.float32), axis=-1)
    greatest_logits = lax.pmax(local_best, ("seq", "exp")).reshape(steps, requests)
    return (hidden_norms, greatest_logits)


def solution(mesh):
    in_specs = (
        P(),
        P(),
        P(),
        P(),
        P(("seq", "exp"), None),
        P(),
        P(None, "seq"),
        P(None, "seq"),
        P(None, "seq"),
        P("seq", None),
        P("exp", "seq", None),
        P("exp", "seq", None),
        P(),
        P(),
        P(("seq", "exp"), None, None),
        P(("seq", "exp"), None, None),
        P(("seq", "exp"), None, None),
        P(None, "exp"),
        P(None, "exp"),
        P("exp", None),
        P(),
        P(None, ("seq", "exp")),
    )
    out_specs = (P(), P())
    return jax.shard_map(
        on_device, mesh=mesh, in_specs=in_specs, out_specs=out_specs, check_vma=False
    )
```

profile of v0, /device:TPU:0, one launch (start us, length us, event | category | flops | bytes accessed | tf_op | source)
XLA Modules:
  0.0 482.6 jit_solution(16864006460640909355)
XLA Ops:
  7.2 0.8 broadcast_subtract_fusion
  8.1 0.1 sub.51
  8.1 4.9 %convolution_convert_fusion = bf16[128,2048]{1,0:T(8,128)(2,1)} fusion(bf16[1600,2048]{1,0:T(8,128)(2,1)} %param.26, s32[128]{0:T(128)S(1)} %sub.51), kind=kOutput, calls=%fused_computation.8 | convolution fusion | flops 839327744 | bytes 7078400 | tf_op jit(solution)/shard_map/dot_general | solution.py:79
  13.1 0.8 dynamic-slice_compare_fusion
  14.0 0.1 eq.60
  14.3 4.0 copy.184
  18.2 3.9 copy.185
  22.2 0.1 convert_element_type.91
  22.3 4.0 copy.188
  26.4 0.6 dynamic-slice
  27.6 0.1 multiply_cosine_fusion
  27.7 44.3 %all-reduce.15.cloned.1.call-done = bf16[4,32,2048]{2,1,0:T(8,128)(2,1)} async-done(((bf16[4,32,2048]{2,1,0:T(8,128)(2,1)}), bf16[4,32,2048]{2,1,0:T(8,128)(2,1)}) %all-reduce.15.cloned.1.call-update) | async-done | bytes 524304
  72.0 1.6 constant_dynamic-slice_fusion.3
  73.7 42.0 %all-reduce.7.cloned.1.call-done = bf16[4,4,2048]{2,1,0:T(4,128)(2,1)} async-done(((bf16[4,4,2048]{2,1,0:T(4,128)(2,1)}), bf16[4,4,2048]{2,1,0:T(4,128)(2,1)}) %all-reduce.7.cloned.1.call-update) | async-done | bytes 65552 | tf_op jit(solution)/shard_map/psum | solution.py:85
  115.6 1.0 multiply_reduce_fusion.2
  116.6 0.9 multiply_convert_fusion.2
  117.6 2.4 fusion.78
  120.0 0.7 fusion.79
  120.6 0.1 subtract_convert_fusion.1
  120.8 0.1 pad_maximum_fusion
  120.8 8.2 %all_gather.12 = bf16[16,16,128]{2,0,1:T(8,128)(2,1)S(1)} all-gather(bf16[16,4,128]{2,0,1:T(8,128)(2,1)S(1)} %pad_maximum_fusion), channel_id=1, replica_groups=mesh['seq'=4,'exp'=8] {'seq'}, dimensions={1}, use_global_device_ids=true | all-gather | bytes 81920 | tf_op jit(solution)/shard_map/all_gather | solution.py:102
  129.1 0.1 pad_maximum_fusion.1
  129.1 7.3 %all_gather.13 = bf16[16,16,128]{2,0,1:T(8,128)(2,1)S(1)} all-gather(bf16[16,4,128]{2,0,1:T(8,128)(2,1)S(1)} %pad_maximum_fusion.1), channel_id=1, replica_groups=mesh['seq'=4,'exp'=8] {'seq'}, dimensions={1}, use_global_device_ids=true | all-gather | bytes 81920 | tf_op jit(solution)/shard_map/all_gather | solution.py:103
  136.4 0.2 fusion.48
  136.6 0.2 copy.169
  136.8 0.1 fusion.61
  136.9 0.1 fusion.66
  137.0 0.1 copy.170
  137.1 3.5 select_reduce_fusion
  140.6 15.4 %pmax.14 = f32[4,4,16]{0,2,1:T(8,128)S(1)} all-reduce(f32[4,4,16]{0,2,1:T(8,128)S(1)} %get-tuple-element.21), channel_id=1, replica_groups=mesh['seq'=4,'exp'=8] {'seq'}, use_global_device_ids=true, to_apply=%region_4.5 | all-reduce | flops 256 | bytes 2048 | tf_op jit(solution)/shard_map/pmax | solution.py:127
  156.0 0.3 fusion.37
  156.2 3.5 fusion.21
  159.8 14.9 %psum.37 = bf16[4,4,16]{0,2,1:T(8,128)(2,1)S(1)} all-reduce(bf16[4,4,16]{0,2,1:T(8,128)(2,1)S(1)} %fusion.37), channel_id=1, replica_groups=mesh['seq'=4,'exp'=8] {'seq'}, use_global_device_ids=true, to_apply=%region_8.9 | all-reduce | flops 256 | bytes 1024 | tf_op jit(solution)/shard_map/psum | solution.py:136
  174.8 0.1 copy.176
  174.9 0.2 copy.174
  175.1 2.3 convolution_convert_fusion.2
  177.3 7.4 %all_gather.14 = bf16[16,16,128]{2,0,1:T(8,128)(2,1)S(1)} all-gather(bf16[16,4,128]{2,0,1:T(8,128)(2,1)S(1)} %convolution_convert_fusion.2), channel_id=1, replica_groups=mesh['seq'=4,'exp'=8] {'seq'}, dimensions={1}, use_global_device_ids=true | all-gather | bytes 81920 | tf_op jit(solution)/shard_map/all_gather | solution.py:104
  184.8 0.2 convolution_bitcast_fusion.2
  185.1 16.3 %all-reduce.9.cloned.1.call-done = bf16[4,4,16,128]{3,0,2,1:T(4,128)(2,1)} async-done(((bf16[4,4,16,128]{3,0,2,1:T(4,128)(2,1)}), bf16[4,4,16,128]{3,0,2,1:T(4,128)(2,1)}) %all-reduce.9.cloned.1.call-update) | async-done | bytes 65552 | tf_op jit(solution)/shard_map/psum | solution.py:137
  201.4 0.8 fusion.64
  202.2 1.0 convolution_convert_fusion.1
  203.4 42.5 %all-reduce.11.cloned.1.call-done = bf16[16,2048]{1,0:T(8,128)(2,1)} async-done(((bf16[16,2048]{1,0:T(8,128)(2,1)}), bf16[16,2048]{1,0:T(8,128)(2,1)}) %all-reduce.11.cloned.1.call-update) | async-done | bytes 65552 | tf_op jit(solution)/shard_map/psum | solution.py:159
  245.9 0.9 add_convert_fusion
  246.8 14.7 %all_gather.15 = bf16[4,32,2048]{2,0,1:T(4,128)(2,1)S(1)} all-gather(bf16[4,4,2048]{2,0,1:T(4,128)(2,1)S(1)} %copy.178), channel_id=1, replica_groups=mesh['seq'=4,'exp'=8] {'exp'}, dimensions={1}, use_global_device_ids=true | all-gather | bytes 589824 | tf_op jit(solution)/shard_map/all_gather | solution.py:164
  261.5 0.3 copy.179
  261.9 0.4 multiply_reduce_fusion.1
  262.3 0.1 rsqrt.29
  262.4 0.2 fusion.29
  262.6 6.3 %convolution_bitcast_fusion.1 = f32[8,128,352]{1,2,0:T(8,128)S(1)} fusion(bf16[8,2048,352]{1,2,0:T(8,128)(2,1)} %param.36, bf16[128,2048]{1,0:T(8,128)(2,1)S(1)} %fusion.29), kind=kOutput, calls=%fused_computation.13 | convolution fusion | flops 1476395008 | bytes 13500416 | tf_op jit(solution)/shard_map/nd,jdf->jnf/dot_general | solution.py:188
  268.8 0.3 fusion.27
  269.3 0.1 copy.181
  269.5 18.6 %fusion.11 = bf16[8,128,2048]{2,1,0:T(8,128)(2,1)} fusion(bf16[8,352,2048]{2,1,0:T(8,128)(2,1)} %param.38, bf16[8,2048,352]{1,2,0:T(8,128)(2,1)} %param.37, f32[8,128,352]{1,2,0:T(8,128)S(1)} %convolution_bitcast_fusion.1, bf16[128,2048]{1,0:T(8,128)(2,1)S(1)} %fusion.29), kind=kOutput, calls=%fused_computation.16 | convolution fusion | flops 2954952704 | bytes 29229056 | tf_op jit(solution)/shard_map/jnf,jfd->jnd/dot_general | solution.py:191
  288.1 5.3 %fusion = f32[128,1,2048]{2,1,0:T(1,128)S(1)} fusion(bf16[8,128,1]{0,2,1:T(2,128)(2,1)S(1)} %copy.181, bf16[8,128,2048]{2,1,0:T(8,128)(2,1)} %fusion.11), kind=kOutput, calls=%fused_computation | convolution fusion | flops 4194304 | bytes 5244928 | tf_op jit(solution)/shard_map/jn,jnd->nd/dot_general | solution.py:194
  293.4 0.3 copy.232
  293.8 1.0 copy-done.4
  294.8 0.5 fusion.45
  295.3 3.1 fusion.8
  298.5 1.0 copy-done.3
  299.5 130.2 %all-reduce.13.cloned.1.call-done = f32[128,2048]{1,0:T(8,128)} async-done(((f32[128,2048]{1,0:T(8,128)}), f32[128,2048]{1,0:T(8,128)}) %all-reduce.13.cloned.1.call-update) | async-done | bytes 1048592 | tf_op jit(solution)/shard_map/psum | solution.py:209
  429.7 1.4 bitcast_add_fusion
  431.2 5.0 %convolution_reduce_fusion = f32[128]{0:T(128)S(1)} fusion(bf16[2048,1600]{0,1:T(8,128)(2,1)} %param.43, f32[128,2048]{1,0:T(8,128)S(1)} %get-tuple-element.7, f32[2048]{0:T(1024)S(1)} %copy-done.7, f32[128]{0:T(128)S(1)} %get-tuple-element.19), kind=kOutput, calls=%fused_computation.17 | convolution fusion | flops 839851904 | bytes 7611392 | tf_op jit(solution)/shard_map/dot_general | solution.py:212
  436.2 0.1 reshape.303
  436.3 39.1 %pmax.15 = f32[4,32]{1,0:T(4,128)} all-reduce(f32[4,32]{1,0:T(4,128)S(1)} %reshape.303), channel_id=1, replica_groups=mesh['seq'=4,'exp'=8] {'seq','exp'}, use_global_device_ids=true, to_apply=%region_18.19 | all-reduce | flops 128 | bytes 1024 | tf_op jit(solution)/shard_map/pmax | solution.py:213
  475.4 0.7 sqrt.8
  (59 shorter events, 1.2 us)
Async XLA Ops:
  7.2 195.1 %copy-start = (bf16[512,2048]{1,0:T(8,128)(2,1)S(1)}, bf16[512,2048]{1,0:T(8,128)(2,1)}, u32[]{:S(2)}) copy-start(bf16[512,2048]{1,0:T(8,128)(2,1)} %param.31) | copy-start | bytes 6291460
  7.2 64.8 %all-reduce.15.cloned.1.call-start = ((), (), s32[]{:S(2)}) async-start(), calls=%async_computation.4 | async-start | bytes 1048576
  8.1 5.9 %copy-start.11 = (s32[32]{0:T(128)S(1)}, s32[32]{0:T(128)}, u32[]{:S(2)}) copy-start(s32[32]{0:T(128)} %param.23) | copy-start | bytes 388
  13.0 102.6 %all-reduce.7.cloned.1.call-start = ((), (), s32[]{:S(2)}) async-start(), calls=%async_computation | async-start | bytes 131072 | tf_op jit(solution)/shard_map/psum | solution.py:85
  22.3 4.0 copy-start.8
  22.3 4.1 copy-start.12
  22.3 94.3 %copy-start.10 = (f32[2048]{0:T(1024)S(1)}, f32[2048]{0:T(1024)}, u32[]{:S(2)}) copy-start(f32[2048]{0:T(1024)} %param.27) | copy-start | bytes 24580
  73.6 127.8 %all-reduce.9.cloned.1.call-start = ((), (), s32[]{:S(2)}) async-start(), calls=%async_computation.1 | async-start | bytes 131072 | tf_op jit(solution)/shard_map/psum | solution.py:137
  117.6 2.4 copy-start.2
  159.8 86.1 %all-reduce.11.cloned.1.call-start = ((), (), s32[]{:S(2)}) async-start(), calls=%async_computation.2 | async-start | bytes 131072 | tf_op jit(solution)/shard_map/psum | solution.py:159
  175.1 28.3 %copy-start.5 = (bf16[4,4,2048]{2,1,0:T(4,128)(2,1)S(1)}, bf16[4,4,2048]{2,1,0:T(4,128)(2,1)}, u32[]{:S(2)}) copy-start(bf16[4,4,2048]{2,1,0:T(4,128)(2,1)} %all-reduce.7.cloned.1.call-done) | copy-start | bytes 196612
  203.2 59.1 %copy-start.9 = (f32[2048]{0:T(1024)S(1)}, f32[2048]{0:T(1024)}, u32[]{:S(2)}) copy-start(f32[2048]{0:T(1024)} %param.34) | copy-start | bytes 24580
  203.3 226.5 %all-reduce.13.cloned.1.call-start = ((), (), s32[]{:S(2)}) async-start(), calls=%async_computation.3 | async-start | bytes 2097152 | tf_op jit(solution)/shard_map/psum | solution.py:209
  262.6 6.3 %copy-start.6 = (bf16[2048,64]{0,1:T(8,128)(2,1)S(1)}, bf16[2048,64]{0,1:T(8,128)(2,1)}, u32[]{:S(2)}) copy-start(bf16[2048,64]{0,1:T(8,128)(2,1)} %param.35) | copy-start | bytes 786436
  293.4 1.4 copy-start.4
  298.4 1.0 copy-start.3
  298.5 132.7 %copy-start.7 = (f32[2048]{0:T(1024)S(1)}, f32[2048]{0:T(1024)}, u32[]{:S(2)}) copy-start(f32[2048]{0:T(1024)} %param.42) | copy-start | bytes 24580
  431.2 44.9 %copy-start.1 = (bf16[512,2048]{1,0:T(8,128)(2,1)S(1)}, bf16[512,2048]{1,0:T(8,128)(2,1)}, u32[]{:S(2)}) copy-start(bf16[512,2048]{1,0:T(8,128)(2,1)} %param.31) | copy-start | bytes 6291460
Sparse Core Ops, SparseCore 0:
  13.1 58.8 all-reduce.14
  75.1 40.4 all-reduce.6
  159.9 41.4 all-reduce.8
  204.3 41.4 all-reduce.10
  299.6 130.0 all-reduce.12
where the time goes:
time: 484 us; the launch traced here: 483 us
  waiting for transfers between devices  275 us (57%)
  blocking collectives  107 us (22%)
  matrix products  57.7 us (12%)
  local copies, waits for them, and re-layouts  19.1 us (4%)
  between operations  14.8 us (3%)
  other arithmetic  8.37 us (2%)
    psum x1, waiting for transfers between devices, on_device(): final_hidden = resid_all + lax.psum(term_rows, ('seq', 'exp'))  130 us
    unnamed x6, waiting for transfers between devices  44.4 us
    psum x1, waiting for transfers between devices, on_device(): lax.psum(jnp.dot(own_heads, w_out, preferred_element_type=jnp.float32).as...  42.5 us
    psum x1, waiting for transfers between devices, on_device(): lax.psum(block_part, 'seq').astype(jnp.float32)  42 us
    pmax x1, blocking collectives, on_device(): lax.pmax(local_best, ('seq', 'exp')).reshape(steps, requests)  39.1 us
    dot_general x1, matrix products, on_device(): jnp.einsum('jnf,jfd->jnd', expert_hidden, down_pieces, preferred_element_...  18.6 us
    psum x1, waiting for transfers between devices, on_device(): lax.psum(local_mixture.astype(jnp.bfloat16), 'seq').astype(jnp.float32)  16.3 us
    pmax x1, blocking collectives, on_device(): top_score = lax.pmax(local_top, 'seq')  15.4 us
  transfers between devices with their start and end apart: 5, of which 5 were waited for; matrix products, arithmetic and copies ran while one was open for 3% of the time, Pallas kernels for 0%

commit v1 on v0

--- a/solution.py
+++ b/solution.py
@@ -1,3 +1,4 @@
+import functools
 import math
 import jax
 import jax.numpy as jnp
@@ -9,6 +10,14 @@
 BLK = 16
 epsilon = 1e-06
 negative = -1e30
+
+
+def touch_digits(x_in, peer_axis, chip_axis):
+    mid_arr = lax.psum(lax.psum(x_in, axis_name=peer_axis), axis_name=chip_axis)
+    return mid_arr
+
+
+solve_scenes = functools.partial(touch_digits, peer_axis="exp", chip_axis="seq")
 
 
 def rms_scale(values, scales):
@@ -206,7 +215,7 @@
         share_start,
         0,
     )
-    final_hidden = resid_all + lax.psum(term_rows, ("seq", "exp"))
+    final_hidden = resid_all + solve_scenes(term_rows)
     hidden_norms = jnp.sqrt(jnp.mean(final_hidden * final_hidden, axis=-1)).reshape(steps, requests)
     head_in = rms_scale(final_hidden, final_gain).astype(jnp.bfloat16)
     local_best = jnp.max(jnp.dot(head_in, w_head, preferred_element_type=jnp.float32), axis=-1)

time: 484 us -> 467 us (0.965)
  waiting for transfers between devices: 275 us -> 259 us
    psum x1 -> x2, waiting for transfers between devices: 130 us -> 114 us  [touch_digits(): mid_arr = lax.psum(lax.psum(x_in, axis_name=peer_axis), axis_name=chip_axis)]
    unnamed x6 -> x7, waiting for transfers between devices: 44.4 us -> 44.4 us
  transfers between devices with their start and end apart: 5 -> 6, of which waited for: 5 -> 6; matrix products, arithmetic and copies ran while one was open for 3% -> 4% of each run, Pallas kernels for 0% -> 0%
where the time goes in v1:
time: 467 us; the launch traced here: 466 us
  waiting for transfers between devices  259 us (55%)
  blocking collectives  107 us (23%)
  matrix products  57.7 us (12%)
  local copies, waits for them, and re-layouts  19.1 us (4%)
  between operations  15.1 us (3%)
  other arithmetic  8.37 us (2%)
    psum x2, waiting for transfers between devices, touch_digits(): mid_arr = lax.psum(lax.psum(x_in, axis_name=peer_axis), axis_name=chip_axis)  114 us
    unnamed x7, waiting for transfers between devices  44.4 us
    psum x1, waiting for transfers between devices, on_device(): lax.psum(jnp.dot(own_heads, w_out, preferred_element_type=jnp.float32).as...  42.5 us
    psum x1, waiting for transfers between devices, on_device(): lax.psum(block_part, 'seq').astype(jnp.float32)  42 us
    pmax x1, blocking collectives, on_device(): lax.pmax(local_best, ('seq', 'exp')).reshape(steps, requests)  39.3 us
    dot_general x1, matrix products, on_device(): jnp.einsum('jnf,jfd->jnd', expert_hidden, down_pieces, preferred_element_...  18.6 us
    psum x1, waiting for transfers between devices, on_device(): lax.psum(local_mixture.astype(jnp.bfloat16), 'seq').astype(jnp.float32)  16.3 us
    pmax x1, blocking collectives, on_device(): top_score = lax.pmax(local_top, 'seq')  15.4 us
  transfers between devices with their start and end apart: 6, of which 6 were waited for; matrix products, arithmetic and copies ran while one was open for 4% of the time, Pallas kernels for 0%

profile of v1, /device:TPU:0, one launch (start us, length us, event | category | flops | bytes accessed | tf_op | source)
XLA Modules:
  0.0 466.4 jit_solution(5940974945236457855)
XLA Ops:
  7.2 0.8 broadcast_subtract_fusion
  8.1 0.1 sub.51
  8.1 4.9 %convolution_convert_fusion = bf16[128,2048]{1,0:T(8,128)(2,1)} fusion(bf16[1600,2048]{1,0:T(8,128)(2,1)} %param.26, s32[128]{0:T(128)S(1)} %sub.51), kind=kOutput, calls=%fused_computation.8 | convolution fusion | flops 839327744 | bytes 7078400 | tf_op jit(solution)/shard_map/dot_general | solution.py:88
  13.1 0.8 dynamic-slice_compare_fusion
  14.0 0.1 eq.60
  14.3 4.0 copy.184
  18.2 3.9 copy.185
  22.2 0.1 convert_element_type.91
  22.3 4.0 copy.188
  26.4 0.6 dynamic-slice
  27.6 0.1 multiply_cosine_fusion
  27.7 44.3 %all-reduce.18.cloned.1.call-done = bf16[4,32,2048]{2,1,0:T(8,128)(2,1)} async-done(((bf16[4,32,2048]{2,1,0:T(8,128)(2,1)}), bf16[4,32,2048]{2,1,0:T(8,128)(2,1)}) %all-reduce.18.cloned.1.call-update) | async-done | bytes 524304
  72.0 1.6 constant_dynamic-slice_fusion.3
  73.7 42.0 %all-reduce.8.cloned.1.call-done = bf16[4,4,2048]{2,1,0:T(4,128)(2,1)} async-done(((bf16[4,4,2048]{2,1,0:T(4,128)(2,1)}), bf16[4,4,2048]{2,1,0:T(4,128)(2,1)}) %all-reduce.8.cloned.1.call-update) | async-done | bytes 65552 | tf_op jit(solution)/shard_map/psum | solution.py:94
  115.6 1.0 multiply_reduce_fusion.2
  116.6 0.9 multiply_convert_fusion.2
  117.6 2.4 fusion.78
  120.0 0.7 fusion.79
  120.6 0.1 subtract_convert_fusion.1
  120.8 0.1 pad_maximum_fusion
  120.8 8.2 %all_gather.12 = bf16[16,16,128]{2,0,1:T(8,128)(2,1)S(1)} all-gather(bf16[16,4,128]{2,0,1:T(8,128)(2,1)S(1)} %pad_maximum_fusion), channel_id=1, replica_groups=mesh['seq'=4,'exp'=8] {'seq'}, dimensions={1}, use_global_device_ids=true | all-gather | bytes 81920 | tf_op jit(solution)/shard_map/all_gather | solution.py:111
  129.1 7.3 %all_gather.13 = bf16[16,16,128]{2,0,1:T(8,128)(2,1)S(1)} all-gather(bf16[16,4,128]{2,0,1:T(8,128)(2,1)S(1)} %pad_maximum_fusion.1), channel_id=1, replica_groups=mesh['seq'=4,'exp'=8] {'seq'}, dimensions={1}, use_global_device_ids=true | all-gather | bytes 81920 | tf_op jit(solution)/shard_map/all_gather | solution.py:112
  136.4 0.2 fusion.48
  136.6 0.2 copy.169
  136.8 0.1 fusion.61
  136.9 0.1 fusion.66
  137.0 0.1 copy.170
  137.1 3.5 select_reduce_fusion
  140.6 15.4 %pmax.14 = f32[4,4,16]{0,2,1:T(8,128)S(1)} all-reduce(f32[4,4,16]{0,2,1:T(8,128)S(1)} %get-tuple-element.21), channel_id=1, replica_groups=mesh['seq'=4,'exp'=8] {'seq'}, use_global_device_ids=true, to_apply=%region_4.5 | all-reduce | flops 256 | bytes 2048 | tf_op jit(solution)/shard_map/pmax | solution.py:136
  156.0 0.3 fusion.37
  156.2 3.5 fusion.21
  159.8 14.9 %psum.44 = bf16[4,4,16]{0,2,1:T(8,128)(2,1)S(1)} all-reduce(bf16[4,4,16]{0,2,1:T(8,128)(2,1)S(1)} %fusion.37), channel_id=1, replica_groups=mesh['seq'=4,'exp'=8] {'seq'}, use_global_device_ids=true, to_apply=%region_8.9 | all-reduce | flops 256 | bytes 1024 | tf_op jit(solution)/shard_map/psum | solution.py:145
  174.8 0.1 copy.176
  174.9 0.2 copy.174
  175.1 2.3 convolution_convert_fusion.2
  177.3 7.4 %all_gather.14 = bf16[16,16,128]{2,0,1:T(8,128)(2,1)S(1)} all-gather(bf16[16,4,128]{2,0,1:T(8,128)(2,1)S(1)} %convolution_convert_fusion.2), channel_id=1, replica_groups=mesh['seq'=4,'exp'=8] {'seq'}, dimensions={1}, use_global_device_ids=true | all-gather | bytes 81920 | tf_op jit(solution)/shard_map/all_gather | solution.py:113
  184.8 0.2 convolution_bitcast_fusion.2
  185.1 16.3 %all-reduce.10.cloned.1.call-done = bf16[4,4,16,128]{3,0,2,1:T(4,128)(2,1)} async-done(((bf16[4,4,16,128]{3,0,2,1:T(4,128)(2,1)}), bf16[4,4,16,128]{3,0,2,1:T(4,128)(2,1)}) %all-reduce.10.cloned.1.call-update) | async-done | bytes 65552 | tf_op jit(solution)/shard_map/psum | solution.py:146
  201.4 0.8 fusion.64
  202.2 1.0 convolution_convert_fusion.1
  203.4 42.5 %all-reduce.12.cloned.1.call-done = bf16[16,2048]{1,0:T(8,128)(2,1)} async-done(((bf16[16,2048]{1,0:T(8,128)(2,1)}), bf16[16,2048]{1,0:T(8,128)(2,1)}) %all-reduce.12.cloned.1.call-update) | async-done | bytes 65552 | tf_op jit(solution)/shard_map/psum | solution.py:168
  245.9 0.9 add_convert_fusion
  246.8 14.7 %all_gather.15 = bf16[4,32,2048]{2,0,1:T(4,128)(2,1)S(1)} all-gather(bf16[4,4,2048]{2,0,1:T(4,128)(2,1)S(1)} %copy.178), channel_id=1, replica_groups=mesh['seq'=4,'exp'=8] {'exp'}, dimensions={1}, use_global_device_ids=true | all-gather | bytes 589824 | tf_op jit(solution)/shard_map/all_gather | solution.py:173
  261.5 0.3 copy.179
  261.9 0.4 multiply_reduce_fusion.1
  262.3 0.1 rsqrt.29
  262.4 0.2 fusion.29
  262.6 6.3 %convolution_bitcast_fusion.1 = f32[8,128,352]{1,2,0:T(8,128)S(1)} fusion(bf16[8,2048,352]{1,2,0:T(8,128)(2,1)} %param.36, bf16[128,2048]{1,0:T(8,128)(2,1)S(1)} %fusion.29), kind=kOutput, calls=%fused_computation.13 | convolution fusion | flops 1476395008 | bytes 13500416 | tf_op jit(solution)/shard_map/nd,jdf->jnf/dot_general | solution.py:197
  268.8 0.3 fusion.27
  269.3 0.1 copy.181
  269.5 18.6 %fusion.11 = bf16[8,128,2048]{2,1,0:T(8,128)(2,1)} fusion(bf16[8,352,2048]{2,1,0:T(8,128)(2,1)} %param.38, bf16[8,2048,352]{1,2,0:T(8,128)(2,1)} %param.37, f32[8,128,352]{1,2,0:T(8,128)S(1)} %convolution_bitcast_fusion.1, bf16[128,2048]{1,0:T(8,128)(2,1)S(1)} %fusion.29), kind=kOutput, calls=%fused_computation.16 | convolution fusion | flops 2954952704 | bytes 29229056 | tf_op jit(solution)/shard_map/jnf,jfd->jnd/dot_general | solution.py:200
  288.1 5.3 %fusion = f32[128,1,2048]{2,1,0:T(1,128)S(1)} fusion(bf16[8,128,1]{0,2,1:T(2,128)(2,1)S(1)} %copy.181, bf16[8,128,2048]{2,1,0:T(8,128)(2,1)} %fusion.11), kind=kOutput, calls=%fused_computation | convolution fusion | flops 4194304 | bytes 5244928 | tf_op jit(solution)/shard_map/jn,jnd->nd/dot_general | solution.py:203
  293.4 0.3 copy.232
  293.8 1.0 copy-done.4
  294.8 0.5 fusion.45
  295.3 3.1 fusion.8
  298.5 1.0 copy-done.3
  299.6 59.1 %all-reduce.14.cloned.1.call-done = f32[128,2048]{1,0:T(8,128)} async-done(((f32[128,2048]{1,0:T(8,128)}), f32[128,2048]{1,0:T(8,128)}) %all-reduce.14.cloned.1.call-update) | async-done | bytes 1048592 | tf_op jit(solution)/shard_map/psum | solution.py:16
  358.7 54.4 %all-reduce.16.cloned.1.call-done = f32[128,2048]{1,0:T(8,128)} async-done(((f32[128,2048]{1,0:T(8,128)}), f32[128,2048]{1,0:T(8,128)}) %all-reduce.16.cloned.1.call-update) | async-done | bytes 1048592 | tf_op jit(solution)/shard_map/psum | solution.py:16
  413.1 1.4 bitcast_add_fusion
  414.6 5.0 %convolution_reduce_fusion = f32[128]{0:T(128)S(1)} fusion(bf16[2048,1600]{0,1:T(8,128)(2,1)} %param.43, f32[128,2048]{1,0:T(8,128)S(1)} %get-tuple-element.7, f32[2048]{0:T(1024)S(1)} %copy-done.7, f32[128]{0:T(128)S(1)} %get-tuple-element.19), kind=kOutput, calls=%fused_computation.17 | convolution fusion | flops 839851904 | bytes 7611392 | tf_op jit(solution)/shard_map/dot_general | solution.py:221
  419.6 0.1 reshape.303
  419.7 39.3 %pmax.15 = f32[4,32]{1,0:T(4,128)} all-reduce(f32[4,32]{1,0:T(4,128)S(1)} %reshape.303), channel_id=1, replica_groups=mesh['seq'=4,'exp'=8] {'seq','exp'}, use_global_device_ids=true, to_apply=%region_19.20 | all-reduce | flops 128 | bytes 1024 | tf_op jit(solution)/shard_map/pmax | solution.py:222
  458.9 0.7 sqrt.8
  (62 shorter events, 1.3 us)
Async XLA Ops:
  7.2 195.1 %copy-start = (bf16[512,2048]{1,0:T(8,128)(2,1)S(1)}, bf16[512,2048]{1,0:T(8,128)(2,1)}, u32[]{:S(2)}) copy-start(bf16[512,2048]{1,0:T(8,128)(2,1)} %param.31) | copy-start | bytes 6291460
  7.2 64.8 %all-reduce.18.cloned.1.call-start = ((), (), s32[]{:S(2)}) async-start(), calls=%async_computation.5 | async-start | bytes 1048576
  8.1 5.9 %copy-start.11 = (s32[32]{0:T(128)S(1)}, s32[32]{0:T(128)}, u32[]{:S(2)}) copy-start(s32[32]{0:T(128)} %param.23) | copy-start | bytes 388
  13.0 102.6 %all-reduce.8.cloned.1.call-start = ((), (), s32[]{:S(2)}) async-start(), calls=%async_computation | async-start | bytes 131072 | tf_op jit(solution)/shard_map/psum | solution.py:94
  22.3 4.0 copy-start.8
  22.3 4.1 copy-start.12
  22.3 94.3 %copy-start.10 = (f32[2048]{0:T(1024)S(1)}, f32[2048]{0:T(1024)}, u32[]{:S(2)}) copy-start(f32[2048]{0:T(1024)} %param.27) | copy-start | bytes 24580
  73.6 127.8 %all-reduce.10.cloned.1.call-start = ((), (), s32[]{:S(2)}) async-start(), calls=%async_computation.1 | async-start | bytes 131072 | tf_op jit(solution)/shard_map/psum | solution.py:146
  117.6 2.4 copy-start.2
  159.8 86.1 %all-reduce.12.cloned.1.call-start = ((), (), s32[]{:S(2)}) async-start(), calls=%async_computation.2 | async-start | bytes 131072 | tf_op jit(solution)/shard_map/psum | solution.py:168
  175.1 28.3 %copy-start.5 = (bf16[4,4,2048]{2,1,0:T(4,128)(2,1)S(1)}, bf16[4,4,2048]{2,1,0:T(4,128)(2,1)}, u32[]{:S(2)}) copy-start(bf16[4,4,2048]{2,1,0:T(4,128)(2,1)} %all-reduce.8.cloned.1.call-done) | copy-start | bytes 196612
  203.2 59.1 %copy-start.9 = (f32[2048]{0:T(1024)S(1)}, f32[2048]{0:T(1024)}, u32[]{:S(2)}) copy-start(f32[2048]{0:T(1024)} %param.34) | copy-start | bytes 24580
  203.3 155.4 %all-reduce.14.cloned.1.call-start = ((), (), s32[]{:S(2)}) async-start(), calls=%async_computation.3 | async-start | bytes 2097152 | tf_op jit(solution)/shard_map/psum | solution.py:16
  262.6 6.3 %copy-start.6 = (bf16[2048,64]{0,1:T(8,128)(2,1)S(1)}, bf16[2048,64]{0,1:T(8,128)(2,1)}, u32[]{:S(2)}) copy-start(bf16[2048,64]{0,1:T(8,128)(2,1)} %param.35) | copy-start | bytes 786436
  293.4 1.4 copy-start.4
  298.4 1.0 copy-start.3
  299.5 113.6 %all-reduce.16.cloned.1.call-start = ((), (), s32[]{:S(2)}) async-start(), calls=%async_computation.4 | async-start | bytes 2097152 | tf_op jit(solution)/shard_map/psum | solution.py:16
  358.7 55.9 %copy-start.7 = (f32[2048]{0:T(1024)S(1)}, f32[2048]{0:T(1024)}, u32[]{:S(2)}) copy-start(f32[2048]{0:T(1024)} %param.42) | copy-start | bytes 24580
  414.6 45.0 %copy-start.1 = (bf16[512,2048]{1,0:T(8,128)(2,1)S(1)}, bf16[512,2048]{1,0:T(8,128)(2,1)}, u32[]{:S(2)}) copy-start(bf16[512,2048]{1,0:T(8,128)(2,1)} %param.31) | copy-start | bytes 6291460
Sparse Core Ops, SparseCore 0:
  13.1 58.8 all-reduce.17
  75.1 40.4 all-reduce.7
  159.9 41.4 all-reduce.9
  204.3 41.4 all-reduce.11
  299.6 58.9 all-reduce.13
  361.6 51.4 all-reduce.15
